TPU v7x, 128 devices: a whole 4x4x4 slice. The times are simulated.
128 devices in a mesh: ctx: 32 (over x, y, core), head: 4 (over z).
Axes of the slice: x: 4, y: 4, z: 4, core: 2. Of those that a mesh axis runs over, the one named last changes fastest.
Arguments:
- queries: bfloat16 [32768, 4096], P('ctx', 'head'), may hold values from -4.5 to 4.5
- keys: bfloat16 [32768, 4096], P('ctx', 'head'), may hold values from -6 to 6
- values: bfloat16 [32768, 4096], P('ctx', 'head'), may hold values from -5.5 to 5.5
- row_target: int32 [32768], replicated, may hold values from 0 to 32767, as said below
- seg_doc: int32 [32], replicated, may hold values from 0 to 3, as said below
- mem_gate: float32 [32], P('head'), may hold values from -2 to 2
- out_weight: bfloat16 [4096, 4096], P(None, 'head'), may hold values from -0.09375 to 0.09375
Outputs:
- layer_out: bfloat16 [32768, 4096], P('ctx', 'head')
Inputs may be any that keep to these rules, and one draw needn't show every extreme that they name: `row_target`: a permutation of the token indices; the rows of one ctx shard of the loader order hold at most 48 tokens of any one segment, and exactly 48 of some. `seg_doc`: never falling along the segments, every document present with one or more segments.
All inputs are finite; a program needn't handle non-finite values.
Results may differ from a plain program's by a relative error of at most 0.0051.
Values may be sent and summed in bfloat16 or wider, within the bound.
No kernel may reach another device: no remote copies, remote signals or barrier semaphores. Data moves between devices by JAX's collectives and lax.ppermute only.
A program may use at most 128 MiB of HBM per device.

v0:
```python
import jax
import jax.numpy as jnp
from jax import lax
from jax.sharding import PartitionSpec as P


def feature(inputs):
    return jax.nn.elu(inputs) + 1.0


def per_device(queries, keys, values, row_target, seg_doc, mem_gate, out_weight):
    highest = lax.Precision.HIGHEST
    f32, bf16 = (jnp.float32, jnp.bfloat16)
    n = lax.axis_size("ctx")
    me = lax.axis_index("ctx")
    seg, width = queries.shape
    heads = mem_gate.shape[0]
    dh = width // heads
    cap = seg // n + seg // n // 2
    slots = n * cap
    targets = row_target.reshape(n, seg)
    r_idx = jnp.arange(seg, dtype=jnp.int32)
    o_idx = jnp.arange(n, dtype=jnp.int32)
    s_idx = jnp.arange(slots, dtype=jnp.int32)
    w_idx = jnp.arange(cap, dtype=jnp.int32)
    lower = (r_idx[None, :] < r_idx[:, None]).astype(bf16)
    mine = lax.dynamic_index_in_dim(targets, me, 0, keepdims=False)
    owner = mine // seg
    match = (owner[:, None] == o_idx[None, :]).astype(bf16)
    before = jnp.dot(lower, match, preferred_element_type=f32)
    within = jnp.sum(jnp.where(match > 0, before, 0.0), axis=1).astype(jnp.int32)
    send_slot = owner * cap + within
    slot_row = jnp.sum(jnp.where(send_slot[None, :] == s_idx[:, None], r_idx[None, :], 0), axis=1)
    arrived = targets // seg == me
    rank = jnp.dot(arrived.astype(bf16), lower.T, preferred_element_type=f32).astype(jnp.int32)
    hit = arrived[:, None, :] & (rank[:, None, :] == w_idx[None, :, None])
    pslot = jnp.sum(jnp.where(hit, (targets % seg)[:, None, :], 0), axis=2).reshape(slots)
    count = jnp.sum(arrived.astype(jnp.int32), axis=1)
    valid = (w_idx[None, :] < count[:, None]).reshape(slots)
    tok_slot = jnp.sum(
        jnp.where((pslot[None, :] == r_idx[:, None]) & valid[None, :], s_idx[None, :], 0), axis=1
    )
    doc = seg_doc[me]
    start = jnp.min(jnp.where(seg_doc == doc, o_idx, n))
    score_scale = dh ** (-0.5)
    causal = r_idx[:, None] >= r_idx[None, :]
    head_count = lax.axis_size("head")
    out_cols = out_weight.shape[1]
    bounds = [0, heads // 2, heads]
    weight_rows = out_weight.reshape(head_count, heads, dh, out_cols)
    gate_all = jax.nn.sigmoid(mem_gate)
    shifts = []
    step = 1
    while step < n:
        shifts.append(step)
        step *= 2

    def dispatch(source):
        buffer = jnp.take(source, slot_row, axis=0, mode="clip").reshape(n, cap, width)
        got = lax.all_to_all(buffer, "ctx", 0, 0, tiled=True).reshape(slots, width)
        return jnp.take(got, tok_slot, axis=0, mode="clip").reshape(seg, heads, dh)

    key_all = dispatch(keys)
    value_all = dispatch(values)
    query_all = dispatch(queries)

    def local_attention(query_part, key_part, value_part):
        scores = (
            jnp.einsum("qhd,khd->hqk", query_part, key_part, preferred_element_type=f32)
            * score_scale
        )
        scores = jnp.where(causal[None], scores, -1e30)
        row_max = jnp.max(scores, axis=-1, keepdims=True)
        weights = jnp.exp(scores - row_max)
        probabilities = (weights / jnp.sum(weights, axis=-1, keepdims=True)).astype(bf16)
        return jnp.einsum("hqk,khd->qhd", probabilities, value_part, preferred_element_type=f32)

    def one_group(g, hold):
        first, last = (bounds[g], bounds[g + 1])
        group_heads = last - first
        group_width = group_heads * dh
        cuts = [first + round(group_heads * i / len(shifts)) for i in range(len(shifts) + 1)]
        cuts = [c - first for c in cuts]
        key_heads = key_all[:, first:last]
        value_heads = value_all[:, first:last]
        query_heads = query_all[:, first:last]
        key_feat = feature(key_heads.astype(f32))
        delta_m = jnp.einsum("khd,khe->hde", key_feat, value_heads.astype(f32), precision=highest)
        delta_z = jnp.sum(key_feat, axis=0)
        delta = jnp.concatenate([delta_m, delta_z[:, None, :]], axis=1)
        pieces = []
        total = delta
        for k, step in enumerate(shifts):
            lo, hi = (cuts[k], cuts[k + 1])
            total, operands = lax.optimization_barrier(
                (total, (query_heads[:, lo:hi], key_heads[:, lo:hi], value_heads[:, lo:hi]))
            )
            perm = [(j, j + step) for j in range(n - step)]
            got = lax.ppermute(total, "ctx", perm)
            if hi > lo:
                piece = local_attention(*operands)
                got, piece = lax.optimization_barrier((got, piece))
                pieces.append(piece)
            total = total + jnp.where(me - step >= start, got, jnp.zeros_like(got))
        local_out = jnp.concatenate(pieces, axis=1)
        memory = total - delta
        mem_m = memory[:, :dh, :]
        mem_z = memory[:, dh, :]
        query_feat = feature(query_heads.astype(f32))
        numerator = jnp.einsum("qhd,hde->qhe", query_feat, mem_m, precision=highest)
        denominator = jnp.einsum("qhd,hd->qh", query_feat, mem_z, precision=highest)
        recalled = numerator / jnp.maximum(denominator, 1.0)[..., None]
        gate_value = gate_all[first:last][None, :, None]
        combined = (
            (gate_value * recalled + (1.0 - gate_value) * local_out)
            .astype(bf16)
            .reshape(seg, group_width)
        )
        outgoing = jnp.take(combined, pslot, axis=0, mode="clip").reshape(n, cap, group_width)
        incoming = lax.all_to_all(outgoing, "ctx", 0, 0, tiled=True).reshape(slots, group_width)
        rows = jnp.take(incoming, send_slot, axis=0, mode="clip")
        gathered = lax.all_gather(rows, "head", axis=1, tiled=True)
        part = jnp.dot(
            gathered,
            weight_rows[:, first:last].reshape(head_count * group_width, out_cols),
            preferred_element_type=f32,
        )
        return (part, combined)

    summed, hold = one_group(0, None)
    for g in range(1, len(bounds) - 1):
        part, hold = one_group(g, hold)
        summed = summed + part
    return summed.astype(bf16)


def solution(mesh):
    return jax.shard_map(
        per_device,
        mesh=mesh,
        in_specs=(
            P("ctx", "head"),
            P("ctx", "head"),
            P("ctx", "head"),
            P(),
            P(),
            P("head"),
            P(None, "head"),
        ),
        out_specs=P("ctx", "head"),
        check_vma=False,
    )
```

profile of v0, /device:TPU:1, one launch (start us, length us, event | category | flops | bytes accessed | tf_op | source)
XLA Modules:
  0.0 402.4 jit_solution(4213001769700298006)
XLA Ops:
  9.0 5.8 %gather_fusion.2 = bf16[1536,1024]{1,0:T(8,128)(2,1)} fusion(bf16[1024,1024]{1,0:T(8,128)(2,1)S(1)} %copy-done, s32[2048]{0:T(1024)S(1)} %pad_clamp_fusion.1), kind=kCustom, calls=%fused_computation.2 | custom fusion | bytes 6297600 | tf_op jit(solution)/shard_map/jit(_take)/gather | solution.py:59
  14.8 8.8 %all-to-all-start.1 = ((bf16[32,48,1024]{2,1,0:T(8,128)(2,1)}), bf16[32,48,1024]{2,1,0:T(8,128)(2,1)}, u32[]{:S(2)}, u32[]{:S(2)}) async-start(bf16[32,48,1024]{2,1,0:T(8,128)(2,1)} %bitcast.224), calls=%async_computation.1 | async-start | bytes 6291456 | tf_op jit(solution)/shard_map/all_to_all | solution.py:60
  23.6 5.8 %gather_fusion = bf16[1536,1024]{1,0:T(8,128)(2,1)} fusion(bf16[1024,1024]{1,0:T(8,128)(2,1)S(1)} %copy-done.2, s32[2048]{0:T(1024)S(1)} %pad_clamp_fusion.1), kind=kCustom, calls=%fused_computation | custom fusion | bytes 6297600 | tf_op jit(solution)/shard_map/jit(_take)/gather | solution.py:59
  29.5 34.0 %all-to-all-done.1 = bf16[32,48,1024]{2,1,0:T(8,128)(2,1)} async-done(((bf16[32,48,1024]{2,1,0:T(8,128)(2,1)}), bf16[32,48,1024]{2,1,0:T(8,128)(2,1)}, u32[]{:S(2)}, u32[]{:S(2)}) %all-to-all-start.1) | async-done | bytes 3145760 | tf_op jit(solution)/shard_map/all_to_all | solution.py:60
  71.9 5.8 %gather_fusion.4 = bf16[1536,1024]{1,0:T(8,128)(2,1)} fusion(bf16[1024,1024]{1,0:T(8,128)(2,1)S(1)} %copy-done.3, s32[2048]{0:T(1024)S(1)} %pad_clamp_fusion.1), kind=kCustom, calls=%fused_computation.4 | custom fusion | bytes 6297600 | tf_op jit(solution)/shard_map/jit(_take)/gather | solution.py:59
  79.1 29.2 %all-to-all-done = bf16[32,48,1024]{2,1,0:T(8,128)(2,1)} async-done(((bf16[32,48,1024]{2,1,0:T(8,128)(2,1)}), bf16[32,48,1024]{2,1,0:T(8,128)(2,1)}, u32[]{:S(2)}, u32[]{:S(2)}) %all-to-all-start) | async-done | bytes 3145760 | tf_op jit(solution)/shard_map/all_to_all | solution.py:60
  108.3 5.3 %all-to-all-start.2 = ((bf16[32,48,1024]{2,1,0:T(8,128)(2,1)}), bf16[32,48,1024]{2,1,0:T(8,128)(2,1)S(1)}, u32[]{:S(2)}, u32[]{:S(2)}) async-start(bf16[32,48,1024]{2,1,0:T(8,128)(2,1)} %bitcast.222), calls=%async_computation.2 | async-start | bytes 6291456 | tf_op jit(solution)/shard_map/all_to_all | solution.py:60
  118.1 8.3 %gather_fusion.3 = bf16[1024,1024]{1,0:T(8,128)(2,1)} fusion(bf16[1536,1024]{1,0:T(8,128)(2,1)} %bitcast.6, s32[1024]{0:T(1024)S(1)} %broadcast_clamp_fusion.1), kind=kCustom, calls=%fused_computation.3 | custom fusion | bytes 4198400 | tf_op jit(solution)/shard_map/jit(_take)/gather | solution.py:61
  130.4 8.3 %gather_fusion.1 = bf16[1024,1024]{1,0:T(8,128)(2,1)} fusion(bf16[1536,1024]{1,0:T(8,128)(2,1)} %bitcast.4, s32[1024]{0:T(1024)S(1)} %broadcast_clamp_fusion.1), kind=kCustom, calls=%fused_computation.1 | custom fusion | bytes 4198400 | tf_op jit(solution)/shard_map/jit(_take)/gather | solution.py:61
  155.9 5.3 %gather_fusion.5 = bf16[1024,1024]{1,0:T(8,128)(2,1)} fusion(bf16[1536,1024]{1,0:T(8,128)(2,1)S(1)} %bitcast.215, s32[1024]{0:T(1024)S(1)} %broadcast_clamp_fusion.1), kind=kCustom, calls=%fused_computation.5 | custom fusion | bytes 4198400 | tf_op jit(solution)/shard_map/jit(_take)/gather | solution.py:61
  200.6 6.2 %collective-permute-start.3 = (f32[4,129,128]{2,1,0:T(8,128)S(1)}, f32[4,129,128]{2,1,0:T(8,128)S(1)}, u32[]{:S(2)}, u32[]{:S(2)}) collective-permute-start(f32[4,129,128]{2,1,0:T(8,128)S(1)} %select_add_fusion.5), channel_id=1, source_target_pairs={{0,32},{4,36},{8,40},{12,44},{16,48},{20,52},{24,56},{28,60},{32,6... | collective-permute-start | bytes 792584 | tf_op jit(solution)/shard_map/ppermute | solution.py:99
  210.3 5.5 %collective-permute-start.4 = (f32[4,129,128]{2,1,0:T(8,128)S(1)}, f32[4,129,128]{2,1,0:T(8,128)S(1)}, u32[]{:S(2)}, u32[]{:S(2)}) collective-permute-start(f32[4,129,128]{2,1,0:T(8,128)S(1)} %select_add_fusion.4), channel_id=1, source_target_pairs={{0,64},{4,68},{8,72},{12,76},{16,80},{20,84},{24,88},{28,92},{32,9... | collective-permute-start | bytes 792584 | tf_op jit(solution)/shard_map/ppermute | solution.py:99
  227.5 5.4 %gather_fusion.6 = bf16[1536,512]{1,0:T(8,128)(2,1)} fusion(bf16[1024,512]{1,0:T(8,128)(2,1)S(1)} %copy.61, s32[2048]{0:T(1024)S(1)} %pad_clamp_fusion), kind=kCustom, calls=%fused_computation.6 | custom fusion | bytes 3151872 | tf_op jit(solution)/shard_map/jit(_take)/gather | solution.py:119
  232.9 11.0 %all-to-all-start.3 = ((bf16[32,48,512]{2,1,0:T(8,128)(2,1)}), bf16[32,48,512]{2,1,0:T(8,128)(2,1)S(1)}, u32[]{:S(2)}, u32[]{:S(2)}) async-start(bf16[32,48,512]{2,1,0:T(8,128)(2,1)} %bitcast.39), calls=%async_computation.3 | async-start | bytes 3145728 | tf_op jit(solution)/shard_map/all_to_all | solution.py:120
  249.0 6.0 %collective-permute-start.7 = (f32[4,129,128]{2,1,0:T(8,128)S(1)}, f32[4,129,128]{2,1,0:T(8,128)S(1)}, u32[]{:S(2)}, u32[]{:S(2)}) collective-permute-start(f32[4,129,128]{2,1,0:T(8,128)S(1)} %select_add_fusion.2), channel_id=1, source_target_pairs={{0,16},{4,20},{8,24},{12,28},{16,32},{20,36},{24,40},{28,44},{32,4... | collective-permute-start | bytes 792584 | tf_op jit(solution)/shard_map/ppermute | solution.py:99
  256.7 9.9 %all-to-all-done.3 = bf16[32,48,512]{2,1,0:T(8,128)(2,1)S(1)} async-done(((bf16[32,48,512]{2,1,0:T(8,128)(2,1)}), bf16[32,48,512]{2,1,0:T(8,128)(2,1)S(1)}, u32[]{:S(2)}, u32[]{:S(2)}) %all-to-all-start.3) | async-done | bytes 1572896 | tf_op jit(solution)/shard_map/all_to_all | solution.py:120
  266.6 5.1 %gather_fusion.7 = bf16[1024,512]{1,0:T(8,128)(2,1)} fusion(bf16[1536,512]{1,0:T(8,128)(2,1)S(1)} %bitcast.216, s32[1024]{0:T(1024)S(1)} %broadcast_clamp_fusion), kind=kCustom, calls=%fused_computation.7 | custom fusion | bytes 2101248 | tf_op jit(solution)/shard_map/jit(_take)/gather | solution.py:121
  278.8 6.7 %collective-permute-start.9 = (f32[4,129,128]{2,1,0:T(8,128)S(1)}, f32[4,129,128]{2,1,0:T(8,128)S(1)}, u32[]{:S(2)}, u32[]{:S(2)}) collective-permute-start(f32[4,129,128]{2,1,0:T(8,128)S(1)} %select_add_fusion), channel_id=1, source_target_pairs={{0,64},{4,68},{8,72},{12,76},{16,80},{20,84},{24,88},{28,92},{32,9... | collective-permute-start | bytes 792584 | tf_op jit(solution)/shard_map/ppermute | solution.py:99
  301.4 31.2 %all_to_all.25 = bf16[32,48,512]{2,1,0:T(8,128)(2,1)S(1)} all-to-all(bf16[32,48,512]{2,1,0:T(8,128)(2,1)S(1)} %bitcast.231), channel_id=1, replica_groups=mesh['ctx'=32,'head'=4] {'ctx'}, dimensions={0} | all-to-all | bytes 3145728 | tf_op jit(solution)/shard_map/all_to_all | solution.py:120
  332.6 5.0 %gather_fusion.9 = bf16[1024,512]{1,0:T(8,128)(2,1)} fusion(bf16[1536,512]{1,0:T(8,128)(2,1)S(1)} %bitcast.217, s32[1024]{0:T(1024)S(1)} %broadcast_clamp_fusion), kind=kCustom, calls=%fused_computation.9 | custom fusion | bytes 2101248 | tf_op jit(solution)/shard_map/jit(_take)/gather | solution.py:121
  337.7 6.1 %fusion.164 = (bf16[4,4,128,1024]{3,2,1,0:T(8,128)(2,1)}, bf16[4,4,128,1024]{3,2,1,0:T(8,128)(2,1)}) fusion(bf16[4,8,128,1024]{3,2,1,0:T(8,128)(2,1)} %bitcast.227), kind=kLoop, calls=%fused_computation.258 | loop fusion | bytes 16777216 | tf_op jit(solution)/shard_map/slice | solution.py:125
  343.8 10.6 %fusion.171 = f32[1024,1024]{1,0:T(8,128)} fusion(bf16[1024,2048]{1,0:T(8,128)(2,1)} %all-gather.5.cloned.1.call-done, bf16[2048,1024]{1,0:T(8,128)(2,1)} %bitcast.233), kind=kOutput, calls=%fused_computation.265 | convolution fusion | flops 4294967296 | bytes 12582912 | tf_op jit(solution)/shard_map/dot_general | solution.py:123
  354.4 30.2 %all-gather.7.cloned.1.call-done = bf16[1024,2048]{1,0:T(8,128)(2,1)} async-done(((bf16[1024,512]{1,0:T(8,128)(2,1)}), bf16[1024,2048]{1,0:T(8,128)(2,1)}) %all-gather.7.cloned.1.call-update) | async-done | bytes 4194320 | tf_op jit(solution)/shard_map/all_gather | solution.py:122
  384.5 10.6 %add_convert_fusion = bf16[1024,1024]{1,0:T(8,128)(2,1)} fusion(f32[1024,1024]{1,0:T(8,128)} %fusion.171, bf16[1024,2048]{1,0:T(8,128)(2,1)} %all-gather.7.cloned.1.call-done, bf16[2048,1024]{1,0:T(8,128)(2,1)} %bitcast.232), kind=kOutput, calls=%fused_computation.26 | convolution fusion | flops 4297064448 | bytes 14680064 | tf_op jit(solution)/shard_map/dot_general | solution.py:123
  (179 shorter events, 118.4 us)
Async XLA Ops:
  7.6 61.5 %copy-start.16 = (s32[32,1024]{1,0:T(8,128)}, s32[32,1024]{1,0:T(8,128)S(1)}, u32[]{:S(2)}) copy-start(s32[32,1024]{1,0:T(8,128)S(1)} %reshape.467) | copy-start | bytes 393220
  14.8 48.6 %all-to-all-start.1 = ((bf16[32,48,1024]{2,1,0:T(8,128)(2,1)}), bf16[32,48,1024]{2,1,0:T(8,128)(2,1)}, u32[]{:S(2)}, u32[]{:S(2)}) async-start(bf16[32,48,1024]{2,1,0:T(8,128)(2,1)} %bitcast.224), calls=%async_computation.1 | async-start | bytes 6291456 | tf_op jit(solution)/shard_map/all_to_all | solution.py:60
  29.5 39.0 %copy-start.27 = (s32[32]{0:T(128)S(1)}, s32[32]{0:T(128)}, u32[]{:S(2)}) copy-start(s32[32]{0:T(128)} %param.11) | copy-start | bytes 388
  29.5 42.4 %copy-start.3 = (bf16[1024,1024]{1,0:T(8,128)(2,1)S(1)}, bf16[1024,1024]{1,0:T(8,128)(2,1)}, u32[]{:S(2)}) copy-start(bf16[1024,1024]{1,0:T(8,128)(2,1)} %param.7) | copy-start | bytes 6291460
  63.4 44.9 %all-to-all-start = ((bf16[32,48,1024]{2,1,0:T(8,128)(2,1)}), bf16[32,48,1024]{2,1,0:T(8,128)(2,1)}, u32[]{:S(2)}, u32[]{:S(2)}) async-start(bf16[32,48,1024]{2,1,0:T(8,128)(2,1)} %bitcast.223), calls=%async_computation | async-start | bytes 6291456 | tf_op jit(solution)/shard_map/all_to_all | solution.py:60
  108.3 47.6 %all-to-all-start.2 = ((bf16[32,48,1024]{2,1,0:T(8,128)(2,1)}), bf16[32,48,1024]{2,1,0:T(8,128)(2,1)S(1)}, u32[]{:S(2)}, u32[]{:S(2)}) async-start(bf16[32,48,1024]{2,1,0:T(8,128)(2,1)} %bitcast.222), calls=%async_computation.2 | async-start | bytes 6291456 | tf_op jit(solution)/shard_map/all_to_all | solution.py:60
  167.3 13.4 %collective-permute-start = (f32[4,129,128]{2,1,0:T(8,128)S(1)}, f32[4,129,128]{2,1,0:T(8,128)S(1)}, u32[]{:S(2)}, u32[]{:S(2)}) collective-permute-start(f32[4,129,128]{2,1,0:T(8,128)S(1)} %pad_maximum_fusion), channel_id=1, source_target_pairs={{0,4},{4,8},{8,12},{12,16},{16,20},{20,24},{24,28},{28,32},{32,36}... | collective-permute-start | bytes 792584 | tf_op jit(solution)/shard_map/ppermute | solution.py:99
  171.0 12.9 %collective-permute-start.5 = (f32[4,129,128]{2,1,0:T(8,128)S(1)}, f32[4,129,128]{2,1,0:T(8,128)S(1)}, u32[]{:S(2)}, u32[]{:S(2)}) collective-permute-start(f32[4,129,128]{2,1,0:T(8,128)S(1)} %pad_maximum_fusion.1), channel_id=1, source_target_pairs={{0,4},{4,8},{8,12},{12,16},{16,20},{20,24},{24,28},{28,32},{32,36}... | collective-permute-start | bytes 792584 | tf_op jit(solution)/shard_map/ppermute | solution.py:99
  180.7 9.6 %collective-permute-start.1 = (f32[4,129,128]{2,1,0:T(8,128)S(1)}, f32[4,129,128]{2,1,0:T(8,128)S(1)}, u32[]{:S(2)}, u32[]{:S(2)}) collective-permute-start(f32[4,129,128]{2,1,0:T(8,128)S(1)} %select_add_fusion.7), channel_id=1, source_target_pairs={{0,8},{4,12},{8,16},{12,20},{16,24},{20,28},{24,32},{28,36},{32,40... | collective-permute-start | bytes 792584 | tf_op jit(solution)/shard_map/ppermute | solution.py:99
  183.9 65.1 %collective-permute-start.6 = (f32[4,129,128]{2,1,0:T(8,128)S(1)}, f32[4,129,128]{2,1,0:T(8,128)}, u32[]{:S(2)}, u32[]{:S(2)}) collective-permute-start(f32[4,129,128]{2,1,0:T(8,128)S(1)} %select_add_fusion.3), channel_id=1, source_target_pairs={{0,8},{4,12},{8,16},{12,20},{16,24},{20,28},{24,32},{28,36},{32,40... | collective-permute-start | bytes 792584 | tf_op jit(solution)/shard_map/ppermute | solution.py:99
  190.3 10.3 %collective-permute-start.2 = (f32[4,129,128]{2,1,0:T(8,128)S(1)}, f32[4,129,128]{2,1,0:T(8,128)S(1)}, u32[]{:S(2)}, u32[]{:S(2)}) collective-permute-start(f32[4,129,128]{2,1,0:T(8,128)S(1)} %select_add_fusion.6), channel_id=1, source_target_pairs={{0,16},{4,20},{8,24},{12,28},{16,32},{20,36},{24,40},{28,44},{32,4... | collective-permute-start | bytes 792584 | tf_op jit(solution)/shard_map/ppermute | solution.py:99
  200.6 9.6 %collective-permute-start.3 = (f32[4,129,128]{2,1,0:T(8,128)S(1)}, f32[4,129,128]{2,1,0:T(8,128)S(1)}, u32[]{:S(2)}, u32[]{:S(2)}) collective-permute-start(f32[4,129,128]{2,1,0:T(8,128)S(1)} %select_add_fusion.5), channel_id=1, source_target_pairs={{0,32},{4,36},{8,40},{12,44},{16,48},{20,52},{24,56},{28,60},{32,6... | collective-permute-start | bytes 792584 | tf_op jit(solution)/shard_map/ppermute | solution.py:99
  210.3 8.9 %collective-permute-start.4 = (f32[4,129,128]{2,1,0:T(8,128)S(1)}, f32[4,129,128]{2,1,0:T(8,128)S(1)}, u32[]{:S(2)}, u32[]{:S(2)}) collective-permute-start(f32[4,129,128]{2,1,0:T(8,128)S(1)} %select_add_fusion.4), channel_id=1, source_target_pairs={{0,64},{4,68},{8,72},{12,76},{16,80},{20,84},{24,88},{28,92},{32,9... | collective-permute-start | bytes 792584 | tf_op jit(solution)/shard_map/ppermute | solution.py:99
  232.9 14.0 %copy-start.19 = (bf16[1024,1,128]{0,2,1:T(8,128)(2,1)S(1)}, bf16[1024,1,128]{0,2,1:T(8,128)(2,1)}, u32[]{:S(2)}) copy-start(bf16[1024,1,128]{0,2,1:T(8,128)(2,1)} %get-tuple-element.86) | copy-start | bytes 786436
  232.9 33.7 %all-to-all-start.3 = ((bf16[32,48,512]{2,1,0:T(8,128)(2,1)}), bf16[32,48,512]{2,1,0:T(8,128)(2,1)S(1)}, u32[]{:S(2)}, u32[]{:S(2)}) async-start(bf16[32,48,512]{2,1,0:T(8,128)(2,1)} %bitcast.39), calls=%async_computation.3 | async-start | bytes 3145728 | tf_op jit(solution)/shard_map/all_to_all | solution.py:120
  243.9 99.8 %all-gather.5.cloned.1.call-start = ((), (), s32[]{:S(2)}) async-start(), calls=%async_computation.5 | async-start | bytes 5242880 | tf_op jit(solution)/shard_map/all_gather | solution.py:122
  247.4 9.2 %copy-start.7 = (bf16[1024,1,128]{2,1,0:T(2,128)(2,1)S(1)}, bf16[1024,1,128]{2,1,0:T(2,128)(2,1)}, u32[]{:S(2)}) copy-start(bf16[1024,1,128]{2,1,0:T(2,128)(2,1)} %get-tuple-element.119) | copy-start | bytes 786436
  247.4 9.2 %copy-start.6 = (bf16[1024,1,128]{2,1,0:T(2,128)(2,1)S(1)}, bf16[1024,1,128]{2,1,0:T(2,128)(2,1)}, u32[]{:S(2)}) copy-start(bf16[1024,1,128]{2,1,0:T(2,128)(2,1)} %get-tuple-element.120) | copy-start | bytes 786436
  249.0 22.7 %collective-permute-start.7 = (f32[4,129,128]{2,1,0:T(8,128)S(1)}, f32[4,129,128]{2,1,0:T(8,128)S(1)}, u32[]{:S(2)}, u32[]{:S(2)}) collective-permute-start(f32[4,129,128]{2,1,0:T(8,128)S(1)} %select_add_fusion.2), channel_id=1, source_target_pairs={{0,16},{4,20},{8,24},{12,28},{16,32},{20,36},{24,40},{28,44},{32,4... | collective-permute-start | bytes 792584 | tf_op jit(solution)/shard_map/ppermute | solution.py:99
  271.7 112.8 %all-gather.7.cloned.1.call-start = ((), (), s32[]{:S(2)}) async-start(), calls=%async_computation.6 | async-start | bytes 5242880 | tf_op jit(solution)/shard_map/all_gather | solution.py:122
  271.8 7.0 %collective-permute-start.8 = (f32[4,129,128]{2,1,0:T(8,128)S(1)}, f32[4,129,128]{2,1,0:T(8,128)S(1)}, u32[]{:S(2)}, u32[]{:S(2)}) collective-permute-start(f32[4,129,128]{2,1,0:T(8,128)S(1)} %select_add_fusion.1), channel_id=1, source_target_pairs={{0,32},{4,36},{8,40},{12,44},{16,48},{20,52},{24,56},{28,60},{32,6... | collective-permute-start | bytes 792584 | tf_op jit(solution)/shard_map/ppermute | solution.py:99
  275.1 10.5 %copy-start.25 = (bf16[1024,1,128]{2,0,1:T(8,128)(2,1)S(1)}, bf16[1024,1,128]{2,0,1:T(8,128)(2,1)}, u32[]{:S(2)}) copy-start(bf16[1024,1,128]{2,0,1:T(8,128)(2,1)} %copy.103) | copy-start | bytes 786436
  278.8 11.4 %collective-permute-start.9 = (f32[4,129,128]{2,1,0:T(8,128)S(1)}, f32[4,129,128]{2,1,0:T(8,128)S(1)}, u32[]{:S(2)}, u32[]{:S(2)}) collective-permute-start(f32[4,129,128]{2,1,0:T(8,128)S(1)} %select_add_fusion), channel_id=1, source_target_pairs={{0,64},{4,68},{8,72},{12,76},{16,80},{20,84},{24,88},{28,92},{32,9... | collective-permute-start | bytes 792584 | tf_op jit(solution)/shard_map/ppermute | solution.py:99
  384.5 10.6 %copy-start.1 = (bf16[1024,1024]{1,0:T(8,128)(2,1)S(1)}, bf16[1024,1024]{1,0:T(8,128)(2,1)}, u32[]{:S(2)}) copy-start(bf16[1024,1024]{1,0:T(8,128)(2,1)} %param.9) | copy-start | bytes 6291460
  (22 other events, 92.6 us)
Sparse Core Ops, SparseCore 0:
  271.8 51.0 all-gather.4
  337.8 46.6 all-gather.6
where the time goes:
time: 410 us; the launch traced here: 402 us
  waiting for transfers between devices  112 us (27%)
  local copies, waits for them, and re-layouts  92.6 us (23%)
  starting transfers between devices  73.5 us (18%)
  matrix products  60.1 us (15%)
  blocking collectives  31.2 us (8%)
  between operations  17.9 us (4%)
  other arithmetic  15.3 us (4%)
    all_to_all x3, waiting for transfers between devices, dispatch(): got = lax.all_to_all(buffer, 'ctx', 0, 0, tiled=True).reshape(slots, width)  63.2 us
    ppermute x10, starting transfers between devices, one_group(): got = lax.ppermute(total, 'ctx', perm)  43.3 us
    all_to_all x1, blocking collectives, one_group(): lax.all_to_all(outgoing, 'ctx', 0, 0, tiled=True)  31.2 us
    all_gather x2, waiting for transfers between devices, one_group(): gathered = lax.all_gather(rows, 'head', axis=1, tiled=True)  30.2 us
    gather x4, local copies, waits for them, and re-layouts, dispatch(): return jnp.take(got, tok_slot, axis=0, mode='clip').reshape(seg, heads, dh)  25.9 us
    dot_general x2, matrix products, one_group(): jnp.dot(gathered, weight_rows[:, first:last].reshape(head_count * group_w...  21.2 us
    all_to_all x3, starting transfers between devices, dispatch(): got = lax.all_to_all(buffer, 'ctx', 0, 0, tiled=True).reshape(slots, width)  19.1 us
    gather x3, local copies, waits for them, and re-layouts, dispatch(): jnp.take(source, slot_row, axis=0, mode='clip').reshape(n, cap, width)  17.5 us
  transfers between devices with their start and end apart: 16, of which 9 were waited for; matrix products, arithmetic and copies ran while one was open for 34% of the time, Pallas kernels for 0%

commit v1 on v0

--- a/solution.py
+++ b/solution.py
@@ -119,7 +119,11 @@
         outgoing = jnp.take(combined, pslot, axis=0, mode="clip").reshape(n, cap, group_width)
         incoming = lax.all_to_all(outgoing, "ctx", 0, 0, tiled=True).reshape(slots, group_width)
         rows = jnp.take(incoming, send_slot, axis=0, mode="clip")
-        gathered = lax.all_gather(rows, "head", axis=1, tiled=True)
+        size = lax.axis_size("head")
+        repeats = [size if d == 1 else 1 for d in range(rows.ndim)]
+        gathered = lax.all_to_all(
+            jnp.tile(rows, repeats), "head", split_axis=1, concat_axis=1, tiled=True
+        )
         part = jnp.dot(
             gathered,
             weight_rows[:, first:last].reshape(head_count * group_width, out_cols),

time: 410 us -> 431 us (1.051)
  the two profiles are of different devices: /device:TPU:1 before, /device:TPU:0 now
where the time goes in v1:
time: 431 us; the launch traced here: 423 us
  waiting for transfers between devices  159 us (37%)
  local copies, waits for them, and re-layouts  109 us (25%)
  starting transfers between devices  77.8 us (18%)
  matrix products  59.7 us (14%)
  other arithmetic  13.2 us (3%)
  between operations  4.45 us (1%)
    all_to_all x2, waiting for transfers between devices, one_group(): lax.all_to_all(jnp.tile(rows, repeats), 'head', split_axis=1, concat_axis...  69.8 us
    all_to_all x3, waiting for transfers between devices, dispatch(): got = lax.all_to_all(buffer, 'ctx', 0, 0, tiled=True).reshape(slots, width)  62.9 us
    ppermute x10, starting transfers between devices, one_group(): got = lax.ppermute(total, 'ctx', perm)  40.1 us
    gather x4, local copies, waits for them, and re-layouts, dispatch(): return jnp.take(got, tok_slot, axis=0, mode='clip').reshape(seg, heads, dh)  25.9 us
    all_to_all x2, waiting for transfers between devices, one_group(): lax.all_to_all(outgoing, 'ctx', 0, 0, tiled=True)  25.3 us
    dot_general x2, matrix products, one_group(): jnp.dot(gathered, weight_rows[:, first:last].reshape(head_count * group_w...  20.7 us
    all_to_all x3, starting transfers between devices, dispatch(): got = lax.all_to_all(buffer, 'ctx', 0, 0, tiled=True).reshape(slots, width)  17.8 us
    gather x3, local copies, waits for them, and re-layouts, dispatch(): jnp.take(source, slot_row, axis=0, mode='clip').reshape(n, cap, width)  17.4 us
  transfers between devices with their start and end apart: 17, of which 8 were waited for; matrix products, arithmetic and copies ran while one was open for 33% of the time, Pallas kernels for 0%

profile of v1, /device:TPU:0, one launch (start us, length us, event | category | flops | bytes accessed | tf_op | source)
XLA Modules:
  0.0 422.7 jit_solution(5922814777215444623)
XLA Ops:
  2.5 5.8 %gather_fusion.2 = bf16[1536,1024]{1,0:T(8,128)(2,1)} fusion(bf16[1024,1024]{1,0:T(8,128)(2,1)S(1)} %copy-done, s32[2048]{0:T(1024)S(1)} %pad_clamp_fusion.1), kind=kCustom, calls=%fused_computation.2 | custom fusion | bytes 6297600 | tf_op jit(solution)/shard_map/jit(_take)/gather | solution.py:59
  8.3 7.7 %all-to-all-start.1 = ((bf16[32,48,1024]{2,1,0:T(8,128)(2,1)}), bf16[32,48,1024]{2,1,0:T(8,128)(2,1)}, u32[]{:S(2)}, u32[]{:S(2)}) async-start(bf16[32,48,1024]{2,1,0:T(8,128)(2,1)} %bitcast.225), calls=%async_computation.1 | async-start | bytes 6291456 | tf_op jit(solution)/shard_map/all_to_all | solution.py:60
  16.0 5.8 %gather_fusion = bf16[1536,1024]{1,0:T(8,128)(2,1)} fusion(bf16[1024,1024]{1,0:T(8,128)(2,1)S(1)} %copy-done.2, s32[2048]{0:T(1024)S(1)} %pad_clamp_fusion.1), kind=kCustom, calls=%fused_computation | custom fusion | bytes 6297600 | tf_op jit(solution)/shard_map/jit(_take)/gather | solution.py:59
  21.8 34.1 %all-to-all-done.1 = bf16[32,48,1024]{2,1,0:T(8,128)(2,1)} async-done(((bf16[32,48,1024]{2,1,0:T(8,128)(2,1)}), bf16[32,48,1024]{2,1,0:T(8,128)(2,1)}, u32[]{:S(2)}, u32[]{:S(2)}) %all-to-all-start.1) | async-done | bytes 3145760 | tf_op jit(solution)/shard_map/all_to_all | solution.py:60
  64.2 5.8 %gather_fusion.4 = bf16[1536,1024]{1,0:T(8,128)(2,1)} fusion(bf16[1024,1024]{1,0:T(8,128)(2,1)S(1)} %copy-done.3, s32[2048]{0:T(1024)S(1)} %pad_clamp_fusion.1), kind=kCustom, calls=%fused_computation.4 | custom fusion | bytes 6297600 | tf_op jit(solution)/shard_map/jit(_take)/gather | solution.py:59
  72.0 28.8 %all-to-all-done = bf16[32,48,1024]{2,1,0:T(8,128)(2,1)} async-done(((bf16[32,48,1024]{2,1,0:T(8,128)(2,1)}), bf16[32,48,1024]{2,1,0:T(8,128)(2,1)}, u32[]{:S(2)}, u32[]{:S(2)}) %all-to-all-start) | async-done | bytes 3145760 | tf_op jit(solution)/shard_map/all_to_all | solution.py:60
  110.5 8.3 %gather_fusion.3 = bf16[1024,1024]{1,0:T(8,128)(2,1)} fusion(bf16[1536,1024]{1,0:T(8,128)(2,1)} %bitcast.6, s32[1024]{0:T(1024)S(1)} %broadcast_clamp_fusion.1), kind=kCustom, calls=%fused_computation.3 | custom fusion | bytes 4198400 | tf_op jit(solution)/shard_map/jit(_take)/gather | solution.py:61
  122.7 8.3 %gather_fusion.1 = bf16[1024,1024]{1,0:T(8,128)(2,1)} fusion(bf16[1536,1024]{1,0:T(8,128)(2,1)} %bitcast.4, s32[1024]{0:T(1024)S(1)} %broadcast_clamp_fusion.1), kind=kCustom, calls=%fused_computation.1 | custom fusion | bytes 4198400 | tf_op jit(solution)/shard_map/jit(_take)/gather | solution.py:61
  148.5 5.3 %gather_fusion.5 = bf16[1024,1024]{1,0:T(8,128)(2,1)} fusion(bf16[1536,1024]{1,0:T(8,128)(2,1)S(1)} %bitcast.217, s32[1024]{0:T(1024)S(1)} %broadcast_clamp_fusion.1), kind=kCustom, calls=%fused_computation.5 | custom fusion | bytes 4198400 | tf_op jit(solution)/shard_map/jit(_take)/gather | solution.py:61
  201.2 6.2 %collective-permute-start.8 = (f32[4,129,128]{2,1,0:T(8,128)S(1)}, f32[4,129,128]{2,1,0:T(8,128)S(1)}, u32[]{:S(2)}, u32[]{:S(2)}) collective-permute-start(f32[4,129,128]{2,1,0:T(8,128)S(1)} %select_add_fusion.1), channel_id=1, source_target_pairs={{0,32},{4,36},{8,40},{12,44},{16,48},{20,52},{24,56},{28,60},{32,6... | collective-permute-start | bytes 792584 | tf_op jit(solution)/shard_map/ppermute | solution.py:99
  213.0 5.7 %collective-permute-start.4 = (f32[4,129,128]{2,1,0:T(8,128)S(1)}, f32[4,129,128]{2,1,0:T(8,128)S(1)}, u32[]{:S(2)}, u32[]{:S(2)}) collective-permute-start(f32[4,129,128]{2,1,0:T(8,128)S(1)} %select_add_fusion.4), channel_id=1, source_target_pairs={{0,64},{4,68},{8,72},{12,76},{16,80},{20,84},{24,88},{28,92},{32,9... | collective-permute-start | bytes 792584 | tf_op jit(solution)/shard_map/ppermute | solution.py:99
  231.6 5.4 %gather_fusion.6 = bf16[1536,512]{1,0:T(8,128)(2,1)} fusion(bf16[1024,512]{1,0:T(8,128)(2,1)S(1)} %copy.121, s32[2048]{0:T(1024)S(1)} %pad_clamp_fusion), kind=kCustom, calls=%fused_computation.6 | custom fusion | bytes 3151872 | tf_op jit(solution)/shard_map/jit(_take)/gather | solution.py:119
  253.3 5.4 %gather_fusion.8 = bf16[1536,512]{1,0:T(8,128)(2,1)} fusion(bf16[1024,512]{1,0:T(8,128)(2,1)S(1)} %copy.136, s32[2048]{0:T(1024)S(1)} %pad_clamp_fusion), kind=kCustom, calls=%fused_computation.8 | custom fusion | bytes 3151872 | tf_op jit(solution)/shard_map/jit(_take)/gather | solution.py:119
  258.7 6.3 %all-to-all-done.3 = bf16[32,48,512]{2,1,0:T(8,128)(2,1)S(1)} async-done(((bf16[32,48,512]{2,1,0:T(8,128)(2,1)}), bf16[32,48,512]{2,1,0:T(8,128)(2,1)S(1)}, u32[]{:S(2)}, u32[]{:S(2)}) %all-to-all-start.3) | async-done | bytes 1572896 | tf_op jit(solution)/shard_map/all_to_all | solution.py:120
  273.7 19.1 %all-to-all-done.5 = bf16[32,48,512]{2,1,0:T(8,128)(2,1)} async-done(((bf16[32,48,512]{2,1,0:T(8,128)(2,1)}), bf16[32,48,512]{2,1,0:T(8,128)(2,1)}, u32[]{:S(2)}, u32[]{:S(2)}) %all-to-all-start.5) | async-done | bytes 1572896 | tf_op jit(solution)/shard_map/all_to_all | solution.py:120
  295.1 5.3 %all-to-all-start.4 = ((bf16[1024,4,512]{2,0,1:T(8,128)(2,1)}), bf16[1024,4,512]{2,0,1:T(8,128)(2,1)}, u32[]{:S(2)}, u32[]{:S(2)}) async-start(bf16[1024,4,512]{2,0,1:T(8,128)(2,1)} %tile.4), calls=%async_computation.4 | async-start | bytes 8388608 | tf_op jit(solution)/shard_map/all_to_all | solution.py:124
  300.4 5.6 %gather_fusion.9 = bf16[1024,512]{1,0:T(8,128)(2,1)S(1)} fusion(bf16[1536,512]{1,0:T(8,128)(2,1)} %bitcast.76, s32[1024]{0:T(1024)S(1)} %broadcast_clamp_fusion), kind=kCustom, calls=%fused_computation.9 | custom fusion | bytes 2101248 | tf_op jit(solution)/shard_map/jit(_take)/gather | solution.py:121
  306.0 43.9 %all-to-all-done.4 = bf16[1024,4,512]{2,0,1:T(8,128)(2,1)} async-done(((bf16[1024,4,512]{2,0,1:T(8,128)(2,1)}), bf16[1024,4,512]{2,0,1:T(8,128)(2,1)}, u32[]{:S(2)}, u32[]{:S(2)}) %all-to-all-start.4) | async-done | bytes 4194336 | tf_op jit(solution)/shard_map/all_to_all | solution.py:124
  357.2 6.1 %fusion.164 = (bf16[4,4,128,1024]{3,2,1,0:T(8,128)(2,1)}, bf16[4,4,128,1024]{3,2,1,0:T(8,128)(2,1)}) fusion(bf16[4,8,128,1024]{3,2,1,0:T(8,128)(2,1)} %bitcast.228), kind=kLoop, calls=%fused_computation.258 | loop fusion | bytes 16777216 | tf_op jit(solution)/shard_map/slice | solution.py:129
  363.2 6.4 %copy.122 = bf16[1024,4,512]{0,2,1:T(8,128)(2,1)} copy(bf16[1024,4,512]{2,0,1:T(8,128)(2,1)} %all-to-all-done.4) | data formatting | bytes 8388608 | tf_op jit(solution)/shard_map/all_to_all | solution.py:124
  369.6 10.0 %fusion.171 = f32[1024,1024]{1,0:T(8,128)} fusion(bf16[1024,2048]{0,1:T(8,128)(2,1)} %bitcast.235, bf16[2048,1024]{1,0:T(8,128)(2,1)} %bitcast.237), kind=kOutput, calls=%fused_computation.265 | convolution fusion | flops 4294967296 | bytes 12582912 | tf_op jit(solution)/shard_map/dot_general | solution.py:127
  379.6 25.9 %all-to-all-done.6 = bf16[1024,4,512]{2,0,1:T(8,128)(2,1)} async-done(((bf16[1024,4,512]{2,0,1:T(8,128)(2,1)}), bf16[1024,4,512]{2,0,1:T(8,128)(2,1)}, u32[]{:S(2)}, u32[]{:S(2)}) %all-to-all-start.6) | async-done | bytes 4194336 | tf_op jit(solution)/shard_map/all_to_all | solution.py:124
  405.5 6.3 %copy.137 = bf16[1024,4,512]{0,2,1:T(8,128)(2,1)} copy(bf16[1024,4,512]{2,0,1:T(8,128)(2,1)} %all-to-all-done.6) | data formatting | bytes 8388608 | tf_op jit(solution)/shard_map/all_to_all | solution.py:124
  411.8 10.7 %add_convert_fusion = bf16[1024,1024]{1,0:T(8,128)(2,1)} fusion(f32[1024,1024]{1,0:T(8,128)} %fusion.171, bf16[1024,2048]{0,1:T(8,128)(2,1)} %bitcast.234, bf16[2048,1024]{1,0:T(8,128)(2,1)} %bitcast.236), kind=kOutput, calls=%fused_computation.26 | convolution fusion | flops 4297064448 | bytes 14680064 | tf_op jit(solution)/shard_map/dot_general | solution.py:127
  (192 shorter events, 140.2 us)
Async XLA Ops:
  8.3 7.7 %copy-start.2 = (bf16[1024,1024]{1,0:T(8,128)(2,1)S(1)}, bf16[1024,1024]{1,0:T(8,128)(2,1)}, u32[]{:S(2)}) copy-start(bf16[1024,1024]{1,0:T(8,128)(2,1)} %param.8) | copy-start | bytes 6291460
  8.3 47.6 %all-to-all-start.1 = ((bf16[32,48,1024]{2,1,0:T(8,128)(2,1)}), bf16[32,48,1024]{2,1,0:T(8,128)(2,1)}, u32[]{:S(2)}, u32[]{:S(2)}) async-start(bf16[32,48,1024]{2,1,0:T(8,128)(2,1)} %bitcast.225), calls=%async_computation.1 | async-start | bytes 6291456 | tf_op jit(solution)/shard_map/all_to_all | solution.py:60
  21.7 39.1 %copy-start.31 = (s32[32]{0:T(128)S(1)}, s32[32]{0:T(128)}, u32[]{:S(2)}) copy-start(s32[32]{0:T(128)} %param.11) | copy-start | bytes 388
  21.7 42.4 %copy-start.3 = (bf16[1024,1024]{1,0:T(8,128)(2,1)S(1)}, bf16[1024,1024]{1,0:T(8,128)(2,1)}, u32[]{:S(2)}) copy-start(bf16[1024,1024]{1,0:T(8,128)(2,1)} %param.7) | copy-start | bytes 6291460
  55.9 44.9 %all-to-all-start = ((bf16[32,48,1024]{2,1,0:T(8,128)(2,1)}), bf16[32,48,1024]{2,1,0:T(8,128)(2,1)}, u32[]{:S(2)}, u32[]{:S(2)}) async-start(bf16[32,48,1024]{2,1,0:T(8,128)(2,1)} %bitcast.224), calls=%async_computation | async-start | bytes 6291456 | tf_op jit(solution)/shard_map/all_to_all | solution.py:60
  100.8 47.8 %all-to-all-start.2 = ((bf16[32,48,1024]{2,1,0:T(8,128)(2,1)}), bf16[32,48,1024]{2,1,0:T(8,128)(2,1)S(1)}, u32[]{:S(2)}, u32[]{:S(2)}) async-start(bf16[32,48,1024]{2,1,0:T(8,128)(2,1)} %bitcast.223), calls=%async_computation.2 | async-start | bytes 6291456 | tf_op jit(solution)/shard_map/all_to_all | solution.py:60
  160.2 11.8 %collective-permute-start = (f32[4,129,128]{2,1,0:T(8,128)S(1)}, f32[4,129,128]{2,1,0:T(8,128)S(1)}, u32[]{:S(2)}, u32[]{:S(2)}) collective-permute-start(f32[4,129,128]{2,1,0:T(8,128)S(1)} %pad_maximum_fusion), channel_id=1, source_target_pairs={{0,4},{4,8},{8,12},{12,16},{16,20},{20,24},{24,28},{28,32},{32,36}... | collective-permute-start | bytes 792584 | tf_op jit(solution)/shard_map/ppermute | solution.py:99
  162.7 12.8 %collective-permute-start.5 = (f32[4,129,128]{2,1,0:T(8,128)S(1)}, f32[4,129,128]{2,1,0:T(8,128)S(1)}, u32[]{:S(2)}, u32[]{:S(2)}) collective-permute-start(f32[4,129,128]{2,1,0:T(8,128)S(1)} %pad_maximum_fusion.1), channel_id=1, source_target_pairs={{0,4},{4,8},{8,12},{12,16},{16,20},{20,24},{24,28},{28,32},{32,36}... | collective-permute-start | bytes 792584 | tf_op jit(solution)/shard_map/ppermute | solution.py:99
  172.1 12.4 %collective-permute-start.1 = (f32[4,129,128]{2,1,0:T(8,128)S(1)}, f32[4,129,128]{2,1,0:T(8,128)S(1)}, u32[]{:S(2)}, u32[]{:S(2)}) collective-permute-start(f32[4,129,128]{2,1,0:T(8,128)S(1)} %select_add_fusion.7), channel_id=1, source_target_pairs={{0,8},{4,12},{8,16},{12,20},{16,24},{20,28},{24,32},{28,36},{32,40... | collective-permute-start | bytes 792584 | tf_op jit(solution)/shard_map/ppermute | solution.py:99
  175.5 14.0 %collective-permute-start.6 = (f32[4,129,128]{2,1,0:T(8,128)S(1)}, f32[4,129,128]{2,1,0:T(8,128)S(1)}, u32[]{:S(2)}, u32[]{:S(2)}) collective-permute-start(f32[4,129,128]{2,1,0:T(8,128)S(1)} %select_add_fusion.3), channel_id=1, source_target_pairs={{0,8},{4,12},{8,16},{12,20},{16,24},{20,28},{24,32},{28,36},{32,40... | collective-permute-start | bytes 792584 | tf_op jit(solution)/shard_map/ppermute | solution.py:99
  184.5 11.5 %copy-start.9 = (bf16[1024,1,128]{2,1,0:T(2,128)(2,1)S(1)}, bf16[1024,1,128]{2,1,0:T(2,128)(2,1)}, u32[]{:S(2)}) copy-start(bf16[1024,1,128]{2,1,0:T(2,128)(2,1)} %get-tuple-element.119) | copy-start | bytes 786436
  184.5 12.1 %collective-permute-start.2 = (f32[4,129,128]{2,1,0:T(8,128)S(1)}, f32[4,129,128]{2,1,0:T(8,128)S(1)}, u32[]{:S(2)}, u32[]{:S(2)}) collective-permute-start(f32[4,129,128]{2,1,0:T(8,128)S(1)} %select_add_fusion.6), channel_id=1, source_target_pairs={{0,16},{4,20},{8,24},{12,28},{16,32},{20,36},{24,40},{28,44},{32,4... | collective-permute-start | bytes 792584 | tf_op jit(solution)/shard_map/ppermute | solution.py:99
  189.6 11.5 %collective-permute-start.7 = (f32[4,129,128]{2,1,0:T(8,128)S(1)}, f32[4,129,128]{2,1,0:T(8,128)S(1)}, u32[]{:S(2)}, u32[]{:S(2)}) collective-permute-start(f32[4,129,128]{2,1,0:T(8,128)S(1)} %select_add_fusion.2), channel_id=1, source_target_pairs={{0,16},{4,20},{8,24},{12,28},{16,32},{20,36},{24,40},{28,44},{32,4... | collective-permute-start | bytes 792584 | tf_op jit(solution)/shard_map/ppermute | solution.py:99
  196.6 16.3 %collective-permute-start.3 = (f32[4,129,128]{2,1,0:T(8,128)S(1)}, f32[4,129,128]{2,1,0:T(8,128)S(1)}, u32[]{:S(2)}, u32[]{:S(2)}) collective-permute-start(f32[4,129,128]{2,1,0:T(8,128)S(1)} %select_add_fusion.5), channel_id=1, source_target_pairs={{0,32},{4,36},{8,40},{12,44},{16,48},{20,52},{24,56},{28,60},{32,6... | collective-permute-start | bytes 792584 | tf_op jit(solution)/shard_map/ppermute | solution.py:99
  201.2 7.4 %copy-start.18 = (bf16[1024,1,128]{0,2,1:T(8,128)(2,1)S(1)}, bf16[1024,1,128]{0,2,1:T(8,128)(2,1)}, u32[]{:S(2)}) copy-start(bf16[1024,1,128]{0,2,1:T(8,128)(2,1)} %get-tuple-element.67) | copy-start | bytes 786436
  201.2 17.5 %collective-permute-start.8 = (f32[4,129,128]{2,1,0:T(8,128)S(1)}, f32[4,129,128]{2,1,0:T(8,128)S(1)}, u32[]{:S(2)}, u32[]{:S(2)}) collective-permute-start(f32[4,129,128]{2,1,0:T(8,128)S(1)} %select_add_fusion.1), channel_id=1, source_target_pairs={{0,32},{4,36},{8,40},{12,44},{16,48},{20,52},{24,56},{28,60},{32,6... | collective-permute-start | bytes 792584 | tf_op jit(solution)/shard_map/ppermute | solution.py:99
  213.0 12.4 %collective-permute-start.4 = (f32[4,129,128]{2,1,0:T(8,128)S(1)}, f32[4,129,128]{2,1,0:T(8,128)S(1)}, u32[]{:S(2)}, u32[]{:S(2)}) collective-permute-start(f32[4,129,128]{2,1,0:T(8,128)S(1)} %select_add_fusion.4), channel_id=1, source_target_pairs={{0,64},{4,68},{8,72},{12,76},{16,80},{20,84},{24,88},{28,92},{32,9... | collective-permute-start | bytes 792584 | tf_op jit(solution)/shard_map/ppermute | solution.py:99
  218.8 26.2 %collective-permute-start.9 = (f32[4,129,128]{2,1,0:T(8,128)S(1)}, f32[4,129,128]{2,1,0:T(8,128)}, u32[]{:S(2)}, u32[]{:S(2)}) collective-permute-start(f32[4,129,128]{2,1,0:T(8,128)S(1)} %select_add_fusion), channel_id=1, source_target_pairs={{0,64},{4,68},{8,72},{12,76},{16,80},{20,84},{24,88},{28,92},{32,9... | collective-permute-start | bytes 792584 | tf_op jit(solution)/shard_map/ppermute | solution.py:99
  237.0 28.0 %all-to-all-start.3 = ((bf16[32,48,512]{2,1,0:T(8,128)(2,1)}), bf16[32,48,512]{2,1,0:T(8,128)(2,1)S(1)}, u32[]{:S(2)}, u32[]{:S(2)}) async-start(bf16[32,48,512]{2,1,0:T(8,128)(2,1)} %bitcast.232), calls=%async_computation.3 | async-start | bytes 3145728 | tf_op jit(solution)/shard_map/all_to_all | solution.py:120
  253.3 16.4 %copy-start.24 = (s32[1024]{0:T(1024)S(1)}, s32[1024]{0:T(1024)}, u32[]{:S(2)}) copy-start(s32[1024]{0:T(1024)} %copy-done.23) | copy-start | bytes 12292
  265.0 27.8 %all-to-all-start.5 = ((bf16[32,48,512]{2,1,0:T(8,128)(2,1)}), bf16[32,48,512]{2,1,0:T(8,128)(2,1)}, u32[]{:S(2)}, u32[]{:S(2)}) async-start(bf16[32,48,512]{2,1,0:T(8,128)(2,1)} %bitcast.233), calls=%async_computation.5 | async-start | bytes 3145728 | tf_op jit(solution)/shard_map/all_to_all | solution.py:120
  295.1 54.8 %all-to-all-start.4 = ((bf16[1024,4,512]{2,0,1:T(8,128)(2,1)}), bf16[1024,4,512]{2,0,1:T(8,128)(2,1)}, u32[]{:S(2)}, u32[]{:S(2)}) async-start(bf16[1024,4,512]{2,0,1:T(8,128)(2,1)} %tile.4), calls=%async_computation.4 | async-start | bytes 8388608 | tf_op jit(solution)/shard_map/all_to_all | solution.py:124
  352.1 53.3 %all-to-all-start.6 = ((bf16[1024,4,512]{2,0,1:T(8,128)(2,1)}), bf16[1024,4,512]{2,0,1:T(8,128)(2,1)}, u32[]{:S(2)}, u32[]{:S(2)}) async-start(bf16[1024,4,512]{2,0,1:T(8,128)(2,1)} %tile.5), calls=%async_computation.6 | async-start | bytes 8388608 | tf_op jit(solution)/shard_map/all_to_all | solution.py:124
  411.8 10.7 %copy-start.1 = (bf16[1024,1024]{1,0:T(8,128)(2,1)S(1)}, bf16[1024,1024]{1,0:T(8,128)(2,1)}, u32[]{:S(2)}) copy-start(bf16[1024,1024]{1,0:T(8,128)(2,1)} %param.9) | copy-start | bytes 6291460
  (28 other events, 101.4 us)
